TPU v7x, 128 devices: a whole 4x4x4 slice. The times are simulated.
128 devices in a mesh: dp: 8 (over x, core), eig: 16 (over y, z).
Axes of the slice: x: 4, y: 4, z: 4, core: 2. Of those that a mesh axis runs over, the one named last changes fastest.
Arguments:
- acts: bfloat16 [4096, 8192], P(('dp', 'eig')), may hold values from -6 to 6
- grads: bfloat16 [4096, 8192], P(('dp', 'eig')), may hold values from -6 to 6
- act_basis: bfloat16 [4096, 8192], P('eig'), may hold values from -0.0625 to 0.0625
- grad_basis: bfloat16 [4096, 8192], P('eig'), may hold values from -0.0625 to 0.0625
- eigenvalues: float32 [4096, 4096], P('eig'), may hold values from 0.05 to 20
- query_grads: bfloat16 [32, 256, 4096], P('dp', None, 'eig'), may hold values from -6 to 6
- query_acts: bfloat16 [32, 256, 4096], P('dp'), may hold values from -6 to 6
- cand_local: int32 [8, 16], P('dp'), may hold values from 0 to 7, as said below
- seq_lengths: int32 [8, 8], P('dp'), may hold values from 1 to 128, 512 in all within a row
Outputs:
- scores: float32 [32, 16], P('dp')
Inputs may be any that keep to these rules, and one draw needn't show every extreme that they name: `cand_local`: entry j of an owner's list names a sequence of dp shard j // 2; the 2 entries of one list that name one shard differ. `seq_lengths`: row d lists the lengths of the 8 sequences packed in order in dp shard d's 512 token rows; they sum to 512.
All inputs are finite; a program needn't handle non-finite values.
Results may differ from a plain program's by a relative error of at most 0.006.
Values may be sent and summed in bfloat16 or wider, within the bound.
No kernel may reach another device: no remote copies, remote signals or barrier semaphores. Data moves between devices by JAX's collectives and lax.ppermute only.
A program may use at most 128 MiB of HBM per device.

v0:
```python
import math
import jax
import jax.numpy as jnp
from jax import lax
from jax.sharding import PartitionSpec as P

DAMPING = 0.1


def shards(
    acts,
    grads,
    act_basis,
    grad_basis,
    eigenvalues,
    query_grads,
    query_acts,
    cand_local,
    seq_lengths,
):
    block_width = act_basis.shape[0]
    stacked = jnp.stack([acts, grads])
    shard_rows = lax.all_gather(stacked, "eig", axis=1, tiled=True)
    act_part = jnp.dot(shard_rows[0], act_basis.T, preferred_element_type=jnp.float32)
    grad_part = jnp.dot(shard_rows[1], grad_basis.T, preferred_element_type=jnp.float32)
    rotated = jnp.concatenate([act_part, grad_part], axis=1).astype(jnp.bfloat16)
    act_block = rotated[:, :block_width]
    grad_block = rotated[:, block_width:]
    group_rows = rotated.shape[0]
    seq_count = seq_lengths.shape[1]
    max_len = 2 * group_rows // seq_count
    pick_lists = lax.all_to_all(cand_local, "dp", split_axis=1, concat_axis=0, tiled=True)
    owners = pick_lists.shape[0]
    per_shard = pick_lists.shape[1]
    lengths = seq_lengths[0]
    offsets = jnp.cumsum(lengths) - lengths
    chosen = (
        pick_lists[:, :, None] == jnp.arange(seq_count, dtype=jnp.int32)[None, None, :]
    ).astype(jnp.int32)
    pick_len = jnp.sum(chosen * lengths[None, None, :], axis=2)
    pick_start = jnp.sum(chosen * offsets[None, None, :], axis=2)
    within = jnp.arange(max_len, dtype=jnp.int32)
    is_live = within[None, None, :] < pick_len[:, :, None]
    row_index = jnp.where(is_live, pick_start[:, :, None] + within[None, None, :], 0).reshape(-1)
    live_rows = is_live.reshape(owners, per_shard * max_len, 1)

    def pack_rows(source):
        gathered_rows = jnp.take(source, row_index, axis=0).reshape(
            owners, per_shard * max_len, source.shape[1]
        )
        return jnp.where(live_rows, gathered_rows, jnp.zeros((), jnp.bfloat16))

    grad_pack = pack_rows(grad_block)
    grad_recv, act_narrow = (
        lax.all_to_all(grad_pack, "dp", split_axis=0, concat_axis=0, tiled=True),
        lax.all_to_all(pack_rows(act_block), "dp", split_axis=0, concat_axis=0, tiled=True),
    )
    act_recv = lax.all_gather(act_narrow, "eig", axis=2, tiled=True)
    slot_count = owners * per_shard * max_len
    full_width = query_acts.shape[2]
    grad_flat = grad_recv.reshape(slot_count, block_width).astype(jnp.float32)
    act_flat = act_recv.reshape(slot_count, full_width)
    damped = eigenvalues + DAMPING

    def score_query(query_pair):
        query_grad, query_act = query_pair
        query_outer = jnp.dot(query_grad.T, query_act, preferred_element_type=jnp.float32)
        precond = (query_outer / damped).astype(jnp.bfloat16)
        projected = lax.dot_general(
            act_flat, precond, (((1,), (1,)), ((), ())), preferred_element_type=jnp.float32
        )
        per_token = jnp.sum(projected * grad_flat, axis=1)
        return jnp.sum(per_token.reshape(owners * per_shard, max_len), axis=1)

    partial_sums = lax.map(score_query, (query_grads, query_acts))
    summed = lax.psum(partial_sums, "eig")
    score_scale = 1.0 / (full_width * 4.0 * math.sqrt(query_acts.shape[1]))
    return summed * score_scale


def solution(mesh):
    placed = (
        P(("dp", "eig"), None),
        P(("dp", "eig"), None),
        P("eig", None),
        P("eig", None),
        P("eig", None),
        P("dp", None, "eig"),
        P("dp", None, None),
        P("dp", None),
        P("dp", None),
    )
    return jax.shard_map(
        shards, mesh=mesh, in_specs=placed, out_specs=P("dp", None), check_vma=False
    )
```

profile of v0, /device:TPU:0, one launch (start us, length us, event | category | flops | bytes accessed | tf_op | source)
XLA Modules:
  0.0 384.3 jit_solution(13105366813927029866)
XLA Ops:
  6.5 2.3 pad_maximum_fusion
  9.4 1.3 reduce.3
  11.4 4.4 %all-to-all-start = ((s32[1,8,2]{2,0,1:T(1,128)}), s32[1,8,2]{2,0,1:T(1,128)S(1)}, u32[]{:S(2)}, u32[]{:S(2)}) async-start(s32[1,8,2]{2,0,1:T(1,128)} %bitcast.6), calls=%async_computation | async-start | bytes 8192 | tf_op jit(solution)/shard_map/all_to_all | solution.py:32
  15.8 0.8 reduce-window.8
  17.3 3.7 all-to-all-done
  21.1 0.9 select_reduce_fusion.1
  22.3 101.1 %all-gather.3.cloned.1.call-done = bf16[2,512,8192]{2,1,0:T(8,128)(2,1)} async-done(((bf16[2,32,8192]{2,1,0:T(8,128)(2,1)}), bf16[2,512,8192]{2,1,0:T(8,128)(2,1)}) %all-gather.3.cloned.1.call-update) | async-done | bytes 16777232 | tf_op jit(solution)/shard_map/all_gather | solution.py:23
  123.4 6.9 %fusion.17 = bf16[512,256]{1,0:T(8,128)(2,1)S(1)} fusion(bf16[256,8192]{1,0:T(8,128)(2,1)} %param.15, bf16[2,512,8192]{2,1,0:T(8,128)(2,1)} %all-gather.3.cloned.1.call-done), kind=kOutput, calls=%fused_computation.18 | convolution fusion | flops 2147614720 | bytes 12845056 | tf_op jit(solution)/shard_map/dot_general | solution.py:24
  130.3 7.5 %gather_fusion = bf16[2048,256]{1,0:T(8,128)(2,1)S(1)} fusion(bf16[512,256]{1,0:T(8,128)(2,1)S(1)} %fusion.17, s32[2048]{0:T(1024)S(1)} %fusion.19), kind=kCustom, calls=%fused_computation.clone | custom fusion | bytes 2105344 | tf_op jit(solution)/shard_map/jit(_take)/gather | solution.py:48
  137.8 6.9 %fusion.18 = bf16[512,256]{1,0:T(8,128)(2,1)S(1)} fusion(bf16[256,8192]{1,0:T(8,128)(2,1)} %param.16, bf16[2,512,8192]{2,1,0:T(8,128)(2,1)} %all-gather.3.cloned.1.call-done), kind=kOutput, calls=%fused_computation.19 | convolution fusion | flops 2147614720 | bytes 12845056 | tf_op jit(solution)/shard_map/dot_general | solution.py:25
  144.8 7.5 %gather_fusion.1 = bf16[2048,256]{1,0:T(8,128)(2,1)S(1)} fusion(bf16[512,256]{1,0:T(8,128)(2,1)S(1)} %fusion.18, s32[2048]{0:T(1024)S(1)} %fusion.19), kind=kCustom, calls=%fused_computation.1.clone | custom fusion | bytes 2105344 | tf_op jit(solution)/shard_map/jit(_take)/gather | solution.py:48
  152.7 1.3 broadcast_select_fusion.2
  154.0 20.1 %all_to_all.23 = bf16[8,256,256]{2,1,0:T(8,128)(2,1)} all-to-all(bf16[8,256,256]{2,1,0:T(8,128)(2,1)S(1)} %get-tuple-element.63), channel_id=1, replica_groups=mesh['dp'=8,'eig'=16] {'dp'}, dimensions={0} | all-to-all | bytes 2097152 | tf_op jit(solution)/shard_map/all_to_all | solution.py:56
  174.2 3.6 all-to-all-start.2
  177.7 4.7 %broadcast_add_fusion = f32[256,4096]{1,0:T(8,128)} fusion(f32[256,4096]{1,0:T(8,128)} %param.17), kind=kLoop, calls=%fused_computation.17 | loop fusion | flops 1048576 | bytes 8388608 | tf_op jit(solution)/shard_map/add | solution.py:63
  182.5 11.1 %all-to-all-done.2 = bf16[8,256,256]{2,1,0:T(8,128)(2,1)S(1)} async-done(((bf16[8,256,256]{2,1,0:T(8,128)(2,1)}), bf16[8,256,256]{2,1,0:T(8,128)(2,1)S(1)}, u32[]{:S(2)}, u32[]{:S(2)}) %all-to-all-start.2) | async-done | bytes 1048608 | tf_op jit(solution)/shard_map/all_to_all | solution.py:55
  193.8 1.9 copy.25
  195.7 96.4 %all-gather.5.cloned.1.call-done = bf16[8,256,4096]{2,1,0:T(8,128)(2,1)} async-done(((bf16[8,256,256]{2,1,0:T(8,128)(2,1)}), bf16[8,256,4096]{2,1,0:T(8,128)(2,1)}) %all-gather.5.cloned.1.call-update) | async-done | bytes 16777232 | tf_op jit(solution)/shard_map/all_gather | solution.py:58
  292.1 46.7 %while.10 = (s32[]{:T(128)}, f32[4,16]{1,0:T(4,128)S(1)}, bf16[4,256,256]{2,1,0:T(8,128)(2,1)}, bf16[4,256,4096]{2,1,0:T(8,128)(2,1)}, f32[256,4096]{1,0:T(8,128...) while((s32[]{:T(128)}, f32[4,16]{1,0:T(4,128)S(1)}, ...), condition=%wide.region_6.8_spmd, body=%wide.region_3.7_spmd.sunk | while | flops 4834983936 | bytes 25314592 | solution.py:75
  292.1 11.5 %fusion.30 = f32[2048]{0:T(1024)S(1)} fusion(f32[2048,256]{0,1:T(8,128)} %get-tuple-element.133, bf16[2048,4096]{1,0:T(8,128)(2,1)} %get-tuple-element.132, f32[256,4096]{1,0:T(8,128)} %get-tuple-element.131, bf16[4,256,4096]{2,1,0:T(8,128)(2,1)} %get-tuple-element.130, s32[]{:T(128)} %get-tuple-element.118, bf16[4,256,256]{2,1,0:T(8,128)(2,1)} %get-tuple-element.129), kind=kOutput, calls=%fused_computation.8.clone.1 | convolution fusion | flops 4834981888 | bytes 25306112 | tf_op jit(solution)/shard_map/while/body/eval_jaxpr/dot_general | solution.py:69
  303.7 11.5 %fusion.30 = f32[2048]{0:T(1024)S(1)} fusion(f32[2048,256]{0,1:T(8,128)} %get-tuple-element.133, bf16[2048,4096]{1,0:T(8,128)(2,1)} %get-tuple-element.132, f32[256,4096]{1,0:T(8,128)} %get-tuple-element.131, bf16[4,256,4096]{2,1,0:T(8,128)(2,1)} %get-tuple-element.130, s32[]{:T(128)} %get-tuple-element.118, bf16[4,256,256]{2,1,0:T(8,128)(2,1)} %get-tuple-element.129), kind=kOutput, calls=%fused_computation.8.clone.1 | convolution fusion | flops 4834981888 | bytes 25306112 | tf_op jit(solution)/shard_map/while/body/eval_jaxpr/dot_general | solution.py:69
  315.4 11.5 %fusion.30 = f32[2048]{0:T(1024)S(1)} fusion(f32[2048,256]{0,1:T(8,128)} %get-tuple-element.133, bf16[2048,4096]{1,0:T(8,128)(2,1)} %get-tuple-element.132, f32[256,4096]{1,0:T(8,128)} %get-tuple-element.131, bf16[4,256,4096]{2,1,0:T(8,128)(2,1)} %get-tuple-element.130, s32[]{:T(128)} %get-tuple-element.118, bf16[4,256,256]{2,1,0:T(8,128)(2,1)} %get-tuple-element.129), kind=kOutput, calls=%fused_computation.8.clone.1 | convolution fusion | flops 4834981888 | bytes 25306112 | tf_op jit(solution)/shard_map/while/body/eval_jaxpr/dot_general | solution.py:69
  327.1 11.5 %fusion.30 = f32[2048]{0:T(1024)S(1)} fusion(f32[2048,256]{0,1:T(8,128)} %get-tuple-element.133, bf16[2048,4096]{1,0:T(8,128)(2,1)} %get-tuple-element.132, f32[256,4096]{1,0:T(8,128)} %get-tuple-element.131, bf16[4,256,4096]{2,1,0:T(8,128)(2,1)} %get-tuple-element.130, s32[]{:T(128)} %get-tuple-element.118, bf16[4,256,256]{2,1,0:T(8,128)(2,1)} %get-tuple-element.129), kind=kOutput, calls=%fused_computation.8.clone.1 | convolution fusion | flops 4834981888 | bytes 25306112 | tf_op jit(solution)/shard_map/while/body/eval_jaxpr/dot_general | solution.py:69
  338.7 38.2 %psum.7 = f32[4,16]{1,0:T(4,128)S(1)} all-reduce(f32[4,16]{1,0:T(4,128)S(1)} %get-tuple-element.43), channel_id=1, replica_groups=mesh['dp'=8,'eig'=16] {'eig'}, use_global_device_ids=true, to_apply=%region_7.9 | all-reduce | flops 64 | bytes 512 | tf_op jit(solution)/shard_map/psum | solution.py:76
  (27 shorter events, 4.1 us)
Async XLA Ops:
  6.5 116.9 %all-gather.3.cloned.1.call-start = ((), (), s32[]{:S(2)}) async-start(), calls=%async_computation.3 | async-start | bytes 17825792 | tf_op jit(solution)/shard_map/all_gather | solution.py:23
  11.4 9.7 %all-to-all-start = ((s32[1,8,2]{2,0,1:T(1,128)}), s32[1,8,2]{2,0,1:T(1,128)S(1)}, u32[]{:S(2)}, u32[]{:S(2)}) async-start(s32[1,8,2]{2,0,1:T(1,128)} %bitcast.6), calls=%async_computation | async-start | bytes 8192 | tf_op jit(solution)/shard_map/all_to_all | solution.py:32
  15.8 276.3 %all-gather.5.cloned.1.call-start = ((), (), s32[]{:S(2)}) async-start(), calls=%async_computation.4 | async-start | bytes 17825792 | tf_op jit(solution)/shard_map/all_gather | solution.py:58
  174.2 19.4 %all-to-all-start.2 = ((bf16[8,256,256]{2,1,0:T(8,128)(2,1)}), bf16[8,256,256]{2,1,0:T(8,128)(2,1)S(1)}, u32[]{:S(2)}, u32[]{:S(2)}) async-start(bf16[8,256,256]{2,1,0:T(8,128)(2,1)} %get-tuple-element.62), calls=%async_computation.2 | async-start | bytes 2097152 | tf_op jit(solution)/shard_map/all_to_all | solution.py:55
Sparse Core Ops, SparseCore 0:
  9.5 113.8 all-gather.2
  174.3 117.7 all-gather.4
where the time goes:
time: 385 us; the launch traced here: 384 us
  waiting for transfers between devices  212 us (55%)
  matrix products  59.9 us (16%)
  blocking collectives  58.3 us (15%)
  local copies, waits for them, and re-layouts  18.4 us (5%)
  other arithmetic  13.8 us (4%)
  between operations  13.5 us (4%)
  starting transfers between devices  8.02 us (2%)
    all_gather x1, waiting for transfers between devices, shards(): shard_rows = lax.all_gather(stacked, 'eig', axis=1, tiled=True)  101 us
    all_gather x1, waiting for transfers between devices, shards(): act_recv = lax.all_gather(act_narrow, 'eig', axis=2, tiled=True)  96.4 us
    dot_general x4, matrix products, score_query(): lax.dot_general(act_flat, precond, (((1,), (1,)), ((), ())), preferred_el...  46 us
    psum x1, blocking collectives, shards(): summed = lax.psum(partial_sums, 'eig')  38.2 us
    all_to_all x1, blocking collectives, shards(): lax.all_to_all(pack_rows(act_block), 'dp', split_axis=0, concat_axis=0, t...  20.1 us
    gather x2, local copies, waits for them, and re-layouts, pack_rows(): jnp.take(source, row_index, axis=0)  15 us
    all_to_all x1, waiting for transfers between devices, shards(): lax.all_to_all(grad_pack, 'dp', split_axis=0, concat_axis=0, tiled=True)  11.1 us
  transfers between devices with their start and end apart: 4, of which 4 were waited for; matrix products, arithmetic and copies ran while one was open for 3% of the time, Pallas kernels for 0%

commit v1 on v0

--- a/solution.py
+++ b/solution.py
@@ -73,7 +73,7 @@
         return jnp.sum(per_token.reshape(owners * per_shard, max_len), axis=1)
 
     partial_sums = lax.map(score_query, (query_grads, query_acts))
-    summed = lax.psum(partial_sums, "eig")
+    summed = jnp.sum(lax.all_gather(partial_sums, axis_name="eig"), 0)
     score_scale = 1.0 / (full_width * 4.0 * math.sqrt(query_acts.shape[1]))
     return summed * score_scale
 

time: 385 us -> 369 us (0.958)
  blocking collectives: 58.3 us -> 42.9 us
    psum x1 -> x0, blocking collectives: 38.2 us -> none  [shards(): summed = lax.psum(partial_sums, 'eig')]
    all_gather x0 -> x1, blocking collectives: none -> 22.7 us  [shards(): summed = jnp.sum(lax.all_gather(partial_sums, axis_name='eig'), 0)]
where the time goes in v1:
time: 369 us
  waiting for transfers between devices  212 us (57%)
  matrix products  59.9 us (16%)
  blocking collectives  42.9 us (12%)
  local copies, waits for them, and re-layouts  18.4 us (5%)
  other arithmetic  13.8 us (4%)
  between operations  13.5 us (4%)
  starting transfers between devices  8.02 us (2%)
    all_gather x1, waiting for transfers between devices, shards(): shard_rows = lax.all_gather(stacked, 'eig', axis=1, tiled=True)  101 us
    all_gather x1, waiting for transfers between devices, shards(): act_recv = lax.all_gather(act_narrow, 'eig', axis=2, tiled=True)  96.4 us
    dot_general x4, matrix products, score_query(): lax.dot_general(act_flat, precond, (((1,), (1,)), ((), ())), preferred_el...  46 us
    all_gather x1, blocking collectives, shards(): summed = jnp.sum(lax.all_gather(partial_sums, axis_name='eig'), 0)  22.7 us
    all_to_all x1, blocking collectives, shards(): lax.all_to_all(pack_rows(act_block), 'dp', split_axis=0, concat_axis=0, t...  20.1 us
    gather x2, local copies, waits for them, and re-layouts, pack_rows(): jnp.take(source, row_index, axis=0)  15 us
    all_to_all x1, waiting for transfers between devices, shards(): lax.all_to_all(grad_pack, 'dp', split_axis=0, concat_axis=0, tiled=True)  11.1 us
  transfers between devices with their start and end apart: 4, of which 4 were waited for; matrix products, arithmetic and copies ran while one was open for 3% of the time, Pallas kernels for 0%

profile of v1, /device:TPU:0, one launch (start us, length us, event | category | flops | bytes accessed | tf_op | source)
XLA Modules:
  0.0 368.9 jit_solution(8878516603925922293)
XLA Ops:
  6.5 2.3 pad_maximum_fusion
  9.4 1.3 reduce.4
  11.4 4.4 %all-to-all-start = ((s32[1,8,2]{2,0,1:T(1,128)}), s32[1,8,2]{2,0,1:T(1,128)S(1)}, u32[]{:S(2)}, u32[]{:S(2)}) async-start(s32[1,8,2]{2,0,1:T(1,128)} %bitcast.6), calls=%async_computation | async-start | bytes 8192 | tf_op jit(solution)/shard_map/all_to_all | solution.py:32
  15.8 0.8 reduce-window.8
  17.3 3.7 %all-to-all-done = s32[1,8,2]{2,0,1:T(1,128)S(1)} async-done(((s32[1,8,2]{2,0,1:T(1,128)}), s32[1,8,2]{2,0,1:T(1,128)S(1)}, u32[]{:S(2)}, u32[]{:S(2)}) %all-to-all-start) | async-done | bytes 96 | tf_op jit(solution)/shard_map/all_to_all | solution.py:32
  21.1 0.9 select_reduce_fusion.1
  22.3 101.1 %all-gather.5.cloned.1.call-done = bf16[2,512,8192]{2,1,0:T(8,128)(2,1)} async-done(((bf16[2,32,8192]{2,1,0:T(8,128)(2,1)}), bf16[2,512,8192]{2,1,0:T(8,128)(2,1)}) %all-gather.5.cloned.1.call-update) | async-done | bytes 16777232 | tf_op jit(solution)/shard_map/all_gather | solution.py:23
  123.4 6.9 %fusion.17 = bf16[512,256]{1,0:T(8,128)(2,1)S(1)} fusion(bf16[256,8192]{1,0:T(8,128)(2,1)} %param.15, bf16[2,512,8192]{2,1,0:T(8,128)(2,1)} %all-gather.5.cloned.1.call-done), kind=kOutput, calls=%fused_computation.18 | convolution fusion | flops 2147614720 | bytes 12845056 | tf_op jit(solution)/shard_map/dot_general | solution.py:24
  130.3 7.5 %gather_fusion = bf16[2048,256]{1,0:T(8,128)(2,1)S(1)} fusion(bf16[512,256]{1,0:T(8,128)(2,1)S(1)} %fusion.17, s32[2048]{0:T(1024)S(1)} %fusion.19), kind=kCustom, calls=%fused_computation.clone | custom fusion | bytes 2105344 | tf_op jit(solution)/shard_map/jit(_take)/gather | solution.py:48
  137.8 6.9 %fusion.18 = bf16[512,256]{1,0:T(8,128)(2,1)S(1)} fusion(bf16[256,8192]{1,0:T(8,128)(2,1)} %param.16, bf16[2,512,8192]{2,1,0:T(8,128)(2,1)} %all-gather.5.cloned.1.call-done), kind=kOutput, calls=%fused_computation.19 | convolution fusion | flops 2147614720 | bytes 12845056 | tf_op jit(solution)/shard_map/dot_general | solution.py:25
  144.8 7.5 %gather_fusion.1 = bf16[2048,256]{1,0:T(8,128)(2,1)S(1)} fusion(bf16[512,256]{1,0:T(8,128)(2,1)S(1)} %fusion.18, s32[2048]{0:T(1024)S(1)} %fusion.19), kind=kCustom, calls=%fused_computation.1.clone | custom fusion | bytes 2105344 | tf_op jit(solution)/shard_map/jit(_take)/gather | solution.py:48
  152.7 1.3 broadcast_select_fusion.2
  154.0 20.1 %all_to_all.23 = bf16[8,256,256]{2,1,0:T(8,128)(2,1)} all-to-all(bf16[8,256,256]{2,1,0:T(8,128)(2,1)S(1)} %get-tuple-element.63), channel_id=1, replica_groups=mesh['dp'=8,'eig'=16] {'dp'}, dimensions={0} | all-to-all | bytes 2097152 | tf_op jit(solution)/shard_map/all_to_all | solution.py:56
  174.2 3.6 all-to-all-start.2
  177.7 4.7 %broadcast_add_fusion = f32[256,4096]{1,0:T(8,128)} fusion(f32[256,4096]{1,0:T(8,128)} %param.17), kind=kLoop, calls=%fused_computation.17 | loop fusion | flops 1048576 | bytes 8388608 | tf_op jit(solution)/shard_map/add | solution.py:63
  182.5 11.1 %all-to-all-done.2 = bf16[8,256,256]{2,1,0:T(8,128)(2,1)S(1)} async-done(((bf16[8,256,256]{2,1,0:T(8,128)(2,1)}), bf16[8,256,256]{2,1,0:T(8,128)(2,1)S(1)}, u32[]{:S(2)}, u32[]{:S(2)}) %all-to-all-start.2) | async-done | bytes 1048608 | tf_op jit(solution)/shard_map/all_to_all | solution.py:55
  193.8 1.9 copy.25
  195.7 96.4 %all-gather.7.cloned.1.call-done = bf16[8,256,4096]{2,1,0:T(8,128)(2,1)} async-done(((bf16[8,256,256]{2,1,0:T(8,128)(2,1)}), bf16[8,256,4096]{2,1,0:T(8,128)(2,1)}) %all-gather.7.cloned.1.call-update) | async-done | bytes 16777232 | tf_op jit(solution)/shard_map/all_gather | solution.py:58
  292.1 46.7 %while.10 = (s32[]{:T(128)}, f32[4,16]{1,0:T(4,128)S(1)}, bf16[4,256,256]{2,1,0:T(8,128)(2,1)}, bf16[4,256,4096]{2,1,0:T(8,128)(2,1)}, f32[256,4096]{1,0:T(8,128...) while((s32[]{:T(128)}, f32[4,16]{1,0:T(4,128)S(1)}, ...), condition=%wide.region_6.8_spmd, body=%wide.region_3.7_spmd.sunk | while | flops 4834983936 | bytes 25314592 | solution.py:75
  292.1 11.5 %fusion.30 = f32[2048]{0:T(1024)S(1)} fusion(f32[2048,256]{0,1:T(8,128)} %get-tuple-element.133, bf16[2048,4096]{1,0:T(8,128)(2,1)} %get-tuple-element.132, f32[256,4096]{1,0:T(8,128)} %get-tuple-element.131, bf16[4,256,4096]{2,1,0:T(8,128)(2,1)} %get-tuple-element.130, s32[]{:T(128)} %get-tuple-element.118, bf16[4,256,256]{2,1,0:T(8,128)(2,1)} %get-tuple-element.129), kind=kOutput, calls=%fused_computation.8.clone.1 | convolution fusion | flops 4834981888 | bytes 25306112 | tf_op jit(solution)/shard_map/while/body/eval_jaxpr/dot_general | solution.py:69
  303.7 11.5 %fusion.30 = f32[2048]{0:T(1024)S(1)} fusion(f32[2048,256]{0,1:T(8,128)} %get-tuple-element.133, bf16[2048,4096]{1,0:T(8,128)(2,1)} %get-tuple-element.132, f32[256,4096]{1,0:T(8,128)} %get-tuple-element.131, bf16[4,256,4096]{2,1,0:T(8,128)(2,1)} %get-tuple-element.130, s32[]{:T(128)} %get-tuple-element.118, bf16[4,256,256]{2,1,0:T(8,128)(2,1)} %get-tuple-element.129), kind=kOutput, calls=%fused_computation.8.clone.1 | convolution fusion | flops 4834981888 | bytes 25306112 | tf_op jit(solution)/shard_map/while/body/eval_jaxpr/dot_general | solution.py:69
  315.4 11.5 %fusion.30 = f32[2048]{0:T(1024)S(1)} fusion(f32[2048,256]{0,1:T(8,128)} %get-tuple-element.133, bf16[2048,4096]{1,0:T(8,128)(2,1)} %get-tuple-element.132, f32[256,4096]{1,0:T(8,128)} %get-tuple-element.131, bf16[4,256,4096]{2,1,0:T(8,128)(2,1)} %get-tuple-element.130, s32[]{:T(128)} %get-tuple-element.118, bf16[4,256,256]{2,1,0:T(8,128)(2,1)} %get-tuple-element.129), kind=kOutput, calls=%fused_computation.8.clone.1 | convolution fusion | flops 4834981888 | bytes 25306112 | tf_op jit(solution)/shard_map/while/body/eval_jaxpr/dot_general | solution.py:69
  327.1 11.5 %fusion.30 = f32[2048]{0:T(1024)S(1)} fusion(f32[2048,256]{0,1:T(8,128)} %get-tuple-element.133, bf16[2048,4096]{1,0:T(8,128)(2,1)} %get-tuple-element.132, f32[256,4096]{1,0:T(8,128)} %get-tuple-element.131, bf16[4,256,4096]{2,1,0:T(8,128)(2,1)} %get-tuple-element.130, s32[]{:T(128)} %get-tuple-element.118, bf16[4,256,256]{2,1,0:T(8,128)(2,1)} %get-tuple-element.129), kind=kOutput, calls=%fused_computation.8.clone.1 | convolution fusion | flops 4834981888 | bytes 25306112 | tf_op jit(solution)/shard_map/while/body/eval_jaxpr/dot_general | solution.py:69
  338.7 22.7 %all-gather.1 = f32[16,4,16]{2,1,0:T(4,128)S(1)} all-gather(f32[1,4,16]{2,1,0:T(4,128)S(1)} %bitcast.75), channel_id=2, replica_groups=mesh['dp'=8,'eig'=16] {'eig'}, dimensions={0}, use_global_device_ids=true | all-gather | bytes 4352 | tf_op jit(solution)/shard_map/all_gather | solution.py:76
  (28 shorter events, 4.2 us)
Async XLA Ops:
  6.5 116.9 %all-gather.5.cloned.1.call-start = ((), (), s32[]{:S(2)}) async-start(), calls=%async_computation.3 | async-start | bytes 17825792 | tf_op jit(solution)/shard_map/all_gather | solution.py:23
  11.4 9.7 %all-to-all-start = ((s32[1,8,2]{2,0,1:T(1,128)}), s32[1,8,2]{2,0,1:T(1,128)S(1)}, u32[]{:S(2)}, u32[]{:S(2)}) async-start(s32[1,8,2]{2,0,1:T(1,128)} %bitcast.6), calls=%async_computation | async-start | bytes 8192 | tf_op jit(solution)/shard_map/all_to_all | solution.py:32
  15.8 276.3 %all-gather.7.cloned.1.call-start = ((), (), s32[]{:S(2)}) async-start(), calls=%async_computation.4 | async-start | bytes 17825792 | tf_op jit(solution)/shard_map/all_gather | solution.py:58
  174.2 19.4 %all-to-all-start.2 = ((bf16[8,256,256]{2,1,0:T(8,128)(2,1)}), bf16[8,256,256]{2,1,0:T(8,128)(2,1)S(1)}, u32[]{:S(2)}, u32[]{:S(2)}) async-start(bf16[8,256,256]{2,1,0:T(8,128)(2,1)} %get-tuple-element.62), calls=%async_computation.2 | async-start | bytes 2097152 | tf_op jit(solution)/shard_map/all_to_all | solution.py:55
Sparse Core Ops, SparseCore 0:
  9.5 113.8 all-gather.4
  174.3 117.7 all-gather.6
